TPU v7x, 32 devices: a whole 2x2x4 slice. The times are simulated.
32 devices in a mesh: grp: 2 (over x), blk: 16 (over z, y, core).
Axes of the slice: x: 2, y: 2, z: 4, core: 2. Of those that a mesh axis runs over, the one named last changes fastest.
Arguments:
- tokens: bfloat16 [16384, 1024], P(('grp', 'blk')), parts along dimension 0, may hold values from -6 to 6
- patch_of_row: int32 [16384], P(('grp', 'blk')), parts along dimension 0, may hold values from 0 to 2047, as said below
- latents: bfloat16 [256, 1024], P('blk'), may hold values from -110 to 110
- contrast_gain: bfloat16 [4, 1024], replicated, may hold values from 0.099609375 to 1.8984375
- norm_gain: bfloat16 [1024], replicated, may hold values from 0.099609375 to 1.8984375
- w_query: bfloat16 [1024, 1024], replicated, may hold values from -0.1875 to 0.1875
- w_key: bfloat16 [1024, 1024], replicated, may hold values from -0.1875 to 0.1875
- w_value: bfloat16 [1024, 1024], replicated, may hold values from -0.1875 to 0.1875
- w_out: bfloat16 [1024, 1024], replicated, may hold values from -0.1875 to 0.1875
Outputs:
- new_latents: bfloat16 [512, 1024], P(('grp', 'blk')), parts along dimension 0
There are 2 independent parts, one for each index of `grp`. A program takes and returns all parts, laid end to end along the dimension named above; an argument that names none is the same for every part. Nothing has to cross between parts.
Inputs may be any that keep to these rules, and one draw needn't show every extreme that they name: `patch_of_row`: for each contrast c, rows c * 2048 to (c + 1) * 2048 - 1 name every patch once, and row c * 2048 + s names a patch p with p // 128 == s % 16.
All inputs are finite; a program needn't handle non-finite values.
Results may differ from a plain program's by a relative error of at most 0.0065.
Values may be sent and summed in bfloat16 or wider, within the bound.
No kernel may reach another device: no remote copies, remote signals or barrier semaphores. Data moves between devices by JAX's collectives and lax.ppermute only.
A program may use at most 64 MiB of HBM per device.

v0:
```python
import jax
import jax.numpy as jnp
from jax import lax
from jax.sharding import PartitionSpec as P

HEADS = 16
CONTRASTS = 4


def split_exact(value, upward):
    high = value.astype(jnp.bfloat16)
    rest = value - high.astype(jnp.float32)
    if upward:
        rest = rest + jnp.abs(rest) * 2.0 ** (-8)
    low = rest.astype(jnp.bfloat16)
    return (high, low)


def joined_rows(tokens, patch_of_row, contrast_gain, cycle_size, my_index):
    tok_rows, model_width = tokens.shape
    per_peer = tok_rows // cycle_size
    patches_dev = tok_rows // CONTRASTS
    all_ids = lax.all_gather(patch_of_row, "blk", tiled=True)
    received = lax.all_to_all(
        tokens.reshape(per_peer, cycle_size, model_width),
        "blk",
        split_axis=1,
        concat_axis=1,
        tiled=True,
    )
    received_ids = jnp.transpose(
        lax.dynamic_index_in_dim(
            all_ids.reshape(cycle_size, per_peer, cycle_size), my_index, axis=2, keepdims=False
        )
    )
    source_dev = lax.broadcasted_iota(jnp.int32, (per_peer, cycle_size), 1)
    row_step = lax.broadcasted_iota(jnp.int32, (per_peer, cycle_size), 0)
    slot_index = source_dev * tok_rows + my_index + cycle_size * row_step
    contrast_id = slot_index // (patches_dev * cycle_size)
    target_row = (contrast_id * patches_dev + received_ids - my_index * patches_dev).reshape(
        tok_rows
    )
    inverse = (
        jnp.zeros((tok_rows,), jnp.int32).at[target_row].set(jnp.arange(tok_rows, dtype=jnp.int32))
    )
    arranged = received.reshape(tok_rows, model_width)[inverse].reshape(
        CONTRASTS, patches_dev, model_width
    )
    return jnp.sum(
        arranged.astype(jnp.float32) * contrast_gain.astype(jnp.float32)[:, None, :], axis=0
    )


def local(tokens, patch_of_row, latents, contrast_gain, norm_gain, w_query, w_key, w_value, w_out):
    cycle_size = lax.axis_size("blk")
    my_index = lax.axis_index("blk")
    model_width = tokens.shape[1]
    head_count = HEADS
    head_width = model_width // head_count
    lat_rows = latents.shape[0]
    queries = (
        jnp.dot(latents, w_query, preferred_element_type=jnp.float32) * head_width ** (-0.5)
    ).astype(jnp.bfloat16)
    all_queries = lax.all_gather(queries, "blk", tiled=True)
    all_lat = all_queries.shape[0]
    joined = joined_rows(tokens, patch_of_row, contrast_gain, cycle_size, my_index)
    patches_dev = joined.shape[0]
    inverse_rms = lax.rsqrt(jnp.mean(joined * joined, axis=-1, keepdims=True) + 1e-05)
    normed = (joined * inverse_rms * norm_gain.astype(jnp.float32)).astype(jnp.bfloat16)
    key_rows = jnp.dot(normed, w_key, preferred_element_type=jnp.float32).astype(jnp.bfloat16)
    value_rows = jnp.dot(normed, w_value, preferred_element_type=jnp.float32).astype(jnp.bfloat16)
    key_heads = key_rows.reshape(patches_dev, head_count, head_width)
    value_heads = value_rows.reshape(patches_dev, head_count, head_width)
    query_heads = all_queries.reshape(all_lat, head_count, head_width)
    scores = jnp.einsum("lhd,khd->lhk", query_heads, key_heads, preferred_element_type=jnp.float32)
    maxima = jnp.max(scores, axis=-1)
    max_high, max_low = split_exact(maxima, True)
    shift = max_high.astype(jnp.float32) + max_low.astype(jnp.float32)
    weights = jnp.exp(scores - shift[..., None])
    totals = jnp.sum(weights, axis=-1)
    tot_high, tot_low = split_exact(totals, False)
    summed = jnp.einsum(
        "lhk,khd->lhd",
        weights.astype(jnp.bfloat16),
        value_heads,
        preferred_element_type=jnp.float32,
    )
    stats = jnp.stack([max_high, max_low, tot_high, tot_low], axis=-1).reshape(
        cycle_size, lat_rows, head_count * 4
    )
    payload = jnp.concatenate(
        [summed.astype(jnp.bfloat16).reshape(cycle_size, lat_rows, model_width), stats], axis=-1
    )
    gathered = lax.all_to_all(payload, "blk", split_axis=0, concat_axis=0, tiled=True)
    part_sums = (
        gathered[:, :, :model_width]
        .astype(jnp.float32)
        .reshape(cycle_size, lat_rows, head_count, head_width)
    )
    part_stats = (
        gathered[:, :, model_width:]
        .astype(jnp.float32)
        .reshape(cycle_size, lat_rows, head_count, 4)
    )
    part_max = part_stats[..., 0] + part_stats[..., 1]
    part_tot = part_stats[..., 2] + part_stats[..., 3]
    top = jnp.max(part_max, axis=0)
    factor = jnp.exp(part_max - top[None])
    total = jnp.sum(part_tot * factor, axis=0)
    accum = jnp.sum(part_sums * factor[..., None], axis=0)
    attended = (accum / total[..., None]).reshape(lat_rows, model_width).astype(jnp.bfloat16)
    mixed = latents.astype(jnp.float32) + jnp.dot(
        attended, w_out, preferred_element_type=jnp.float32
    )
    return mixed.astype(jnp.bfloat16)


def solution(mesh):
    in_specs = (
        P(("grp", "blk"), None),
        P(("grp", "blk")),
        P("blk", None),
        P(),
        P(),
        P(),
        P(),
        P(),
        P(),
    )
    out_specs = P(("grp", "blk"), None)
    return jax.shard_map(local, mesh=mesh, in_specs=in_specs, out_specs=out_specs, check_vma=False)
```

profile of v0, /device:TPU:0, one launch (start us, length us, event | category | flops | bytes accessed | tf_op | source)
XLA Modules:
  0.0 122.3 jit_solution(12066292924014967609)
XLA Ops:
  0.0 3.0 %copy.62 = bf16[32,16,1024]{2,0,1:T(8,128)(2,1)} copy(bf16[32,16,1024]{2,1,0:T(8,128)(2,1)} %bitcast.59) | data formatting | bytes 2097152 | tf_op jit(solution)/shard_map/reshape | solution.py:25
  3.0 7.4 %all-to-all-start = ((bf16[32,16,1024]{2,0,1:T(8,128)(2,1)}), bf16[32,16,1024]{2,0,1:T(8,128)(2,1)}, u32[]{:S(2)}, u32[]{:S(2)}) async-start(bf16[32,16,1024]{2,0,1:T(8,128)(2,1)} %copy.62), calls=%async_computation | async-start | bytes 2097152 | tf_op jit(solution)/shard_map/all_to_all | solution.py:24
  10.5 33.5 %all-gather = s32[16,1,512]{2,1,0:T(1,128)S(1)} all-gather(s32[1,1,512]{2,1,0:T(1,128)S(1)} %bitcast.62), channel_id=1, replica_groups=mesh['grp'=2,'blk'=16] {'blk'}, dimensions={0}, use_global_device_ids=true | all-gather | bytes 34816 | tf_op jit(solution)/shard_map/all_gather | solution.py:23
  45.0 2.0 %fusion.5 = bf16[16,1024]{1,0:T(8,128)(2,1)S(1)} fusion(bf16[16,1024]{1,0:T(8,128)(2,1)S(1)} %copy-done.5, bf16[1024,1024]{1,0:T(8,128)(2,1)} %param.14), kind=kOutput, calls=%fused_computation.15 | convolution fusion | flops 33587200 | bytes 2162688 | tf_op jit(solution)/shard_map/dot_general | solution.py:62
  47.0 22.9 %all_gather.7 = bf16[256,1024]{1,0:T(8,128)(2,1)S(1)} all-gather(bf16[16,1024]{1,0:T(8,128)(2,1)S(1)} %fusion.5), channel_id=1, replica_groups=mesh['grp'=2,'blk'=16] {'blk'}, dimensions={0}, use_global_device_ids=true | all-gather | bytes 557056 | tf_op jit(solution)/shard_map/all_gather | solution.py:64
  69.9 1.0 copy.67
  70.9 2.4 %scatter_custom_fusion = s32[512]{0:T(512)S(1)} fusion(s32[512]{0:T(512)S(1)} %bitcast.63, s32[512]{0:T(512)S(1)} %iota.19, s32[]{:T(128)} %constant.15.clone.1), kind=kCustom, calls=%fused_computation.59 | custom fusion | bytes 2052 | tf_op jit(solution)/shard_map/scatter | solution.py:44
  73.4 1.8 %copy.63 = bf16[32,16,1024]{2,1,0:T(8,128)(2,1)S(1)} copy(bf16[32,16,1024]{2,0,1:T(8,128)(2,1)} %all-to-all-done) | data formatting | bytes 2097152 | tf_op jit(solution)/shard_map/all_to_all | solution.py:24
  75.2 2.8 %gather_fusion = bf16[512,1024]{1,0:T(8,128)(2,1)} fusion(bf16[512,1024]{1,0:T(8,128)(2,1)S(1)} %bitcast.53, s32[1024]{0:T(1024)S(1)} %pad_clamp_fusion), kind=kCustom, calls=%fused_computation | custom fusion | bytes 2099200 | tf_op jit(solution)/shard_map/gather | solution.py:46
  78.0 1.5 %fusion = f32[128,1024]{1,0:T(8,128)S(1)} fusion(bf16[4,128,1024]{2,1,0:T(8,128)(2,1)} %bitcast.57, f32[4,1024]{1,0:T(4,128)S(1)} %convert_element_type.140), kind=kLoop, calls=%fused_computation.3 | loop fusion | flops 1441792 | bytes 1589248 | tf_op jit(solution)/shard_map/reduce_sum | solution.py:49
  80.1 0.8 copy.66
  81.0 1.6 %bitcast_reduce_fusion = (f32[256,16]{0,1:T(8,128)S(1)}, f32[16,128,256]{2,1,0:T(8,128)S(1)}) fusion(bf16[128,16,64]{0,2,1:T(8,128)(2,1)} %bitcast.60, bf16[256,16,64]{0,2,1:T(8,128)(2,1)S(1)} %bitcast.58), kind=kOutput, calls=%fused_computation.5 | convolution fusion | flops 67629056 | bytes 2899968 | tf_op jit(solution)/shard_map/lhd,khd->lhk/dot_general | solution.py:75
  82.6 1.3 %copy-done.1 = f32[16,128,256]{2,1,0:T(8,128)} copy-done((f32[16,128,256]{2,1,0:T(8,128)}, f32[16,128,256]{2,1,0:T(8,128)S(1)}, u32[]{:S(2)}) %copy-start.1) | copy-done | bytes 2097176
  84.3 0.5 convolution_convert_fusion.2
  85.0 2.9 %fusion.4 = bf16[256,16,64]{0,2,1:T(8,128)(2,1)} fusion(bf16[128,16,64]{0,2,1:T(8,128)(2,1)S(1)} %bitcast.61, f32[16,128,256]{2,1,0:T(8,128)} %copy-done.1, f32[256,16]{0,1:T(8,128)S(1)} %convert_add_fusion), kind=kOutput, calls=%fused_computation.10 | convolution fusion | flops 68419584 | bytes 2899968 | tf_op jit(solution)/shard_map/lhk,khd->lhd/dot_general | solution.py:82
  88.5 2.0 %copy.69 = bf16[256,16,64]{2,1,0:T(8,128)(2,1)S(1)} copy(bf16[256,16,64]{0,2,1:T(8,128)(2,1)} %fusion.4) | data formatting | bytes 1048576 | tf_op jit(solution)/shard_map/convert_element_type | solution.py:92
  90.5 1.5 %reshape.145 = bf16[16,16,1024]{2,1,0:T(8,128)(2,1)} reshape(bf16[256,16,64]{2,1,0:T(8,128)(2,1)S(1)} %copy.69) | data formatting | bytes 1048576 | tf_op jit(solution)/shard_map/reshape | solution.py:92
  92.0 1.1 pad_maximum_fusion
  93.1 19.8 %all_to_all.10 = bf16[16,16,1088]{2,1,0:T(8,128)(2,1)S(1)} all-to-all(bf16[16,16,1088]{2,1,0:T(8,128)(2,1)S(1)} %pad_maximum_fusion), channel_id=1, replica_groups=mesh['grp'=2,'blk'=16] {'blk'}, dimensions={0} | all-to-all | bytes 1114112 | tf_op jit(solution)/shard_map/all_to_all | solution.py:94
  112.9 0.8 copy-done.2
  114.6 2.0 %mul.113 = f32[16,16,16,64]{3,2,1,0:T(8,128)} broadcast(f32[16,16,16]{2,1,0:T(8,128)S(1)} %copy.72), dimensions={0,1,2} | broadcast | bytes 1064960 | tf_op jit(solution)/shard_map/mul | solution.py:110
  116.5 2.0 %mul.114 = f32[16,16,1024]{2,1,0:T(8,128)S(1)} reshape(f32[16,16,16,64]{3,2,1,0:T(8,128)} %mul.113) | data formatting | bytes 2097152 | tf_op jit(solution)/shard_map/mul | solution.py:110
  118.5 1.2 multiply_reduce_fusion
  119.7 2.6 %fusion.6 = bf16[16,1024]{1,0:T(8,128)(2,1)} fusion(bf16[1024,1024]{1,0:T(8,128)(2,1)} %param.17, bf16[16,1024]{1,0:T(8,128)(2,1)S(1)} %copy-done.5, f32[16,1024]{1,0:T(8,128)S(1)} %multiply_reduce_fusion, f32[16,1024]{1,0:T(8,128)S(1)} %div.36), kind=kOutput, calls=%fused_computation.16 | convolution fusion | flops 33636352 | bytes 2293760 | tf_op jit(solution)/shard_map/dot_general | solution.py:112
  (52 shorter events, 3.5 us)
Async XLA Ops:
  0.0 79.6 %copy-start = (bf16[1024,1024]{1,0:T(8,128)(2,1)S(1)}, bf16[1024,1024]{1,0:T(8,128)(2,1)}, u32[]{:S(2)}) copy-start(bf16[1024,1024]{1,0:T(8,128)(2,1)} %param.15) | copy-start | bytes 6291460
  0.0 10.5 %copy-start.7 = (bf16[1024]{0:T(1024)(128)(2,1)S(1)}, bf16[1024]{0:T(1024)(128)(2,1)}, u32[]{:S(2)}) copy-start(bf16[1024]{0:T(1024)(128)(2,1)} %param.13) | copy-start | bytes 6148
  0.0 10.5 %copy-start.6 = (bf16[4,1024]{1,0:T(4,128)(2,1)S(1)}, bf16[4,1024]{1,0:T(4,128)(2,1)}, u32[]{:S(2)}) copy-start(bf16[4,1024]{1,0:T(4,128)(2,1)} %param.12) | copy-start | bytes 24580
  0.0 10.5 %copy-start.8 = (s32[512]{0:T(512)S(1)}, s32[512]{0:T(512)}, u32[]{:S(2)}) copy-start(s32[512]{0:T(512)} %param.10) | copy-start | bytes 6148
  0.0 45.0 %copy-start.5 = (bf16[16,1024]{1,0:T(8,128)(2,1)S(1)}, bf16[16,1024]{1,0:T(8,128)(2,1)}, u32[]{:S(2)}) copy-start(bf16[16,1024]{1,0:T(8,128)(2,1)} %param.11) | copy-start | bytes 98308
  3.0 70.4 %all-to-all-start = ((bf16[32,16,1024]{2,0,1:T(8,128)(2,1)}), bf16[32,16,1024]{2,0,1:T(8,128)(2,1)}, u32[]{:S(2)}, u32[]{:S(2)}) async-start(bf16[32,16,1024]{2,0,1:T(8,128)(2,1)} %copy.62), calls=%async_computation | async-start | bytes 2097152 | tf_op jit(solution)/shard_map/all_to_all | solution.py:24
  79.5 1.5 %copy-start.4 = (bf16[256,1024]{0,1:T(8,128)(2,1)S(1)}, bf16[256,1024]{0,1:T(8,128)(2,1)}, u32[]{:S(2)}) copy-start(bf16[256,1024]{0,1:T(8,128)(2,1)} %copy.67) | copy-start | bytes 1572868
  81.0 3.3 %copy-start.3 = (bf16[1024,1024]{1,0:T(8,128)(2,1)S(1)}, bf16[1024,1024]{1,0:T(8,128)(2,1)}, u32[]{:S(2)}) copy-start(bf16[1024,1024]{1,0:T(8,128)(2,1)} %param.16) | copy-start | bytes 6291460
  82.6 1.4 %copy-start.1 = (f32[16,128,256]{2,1,0:T(8,128)}, f32[16,128,256]{2,1,0:T(8,128)S(1)}, u32[]{:S(2)}) copy-start(f32[16,128,256]{2,1,0:T(8,128)S(1)} %get-tuple-element.6) | copy-start | bytes 6291460
  112.9 0.8 copy-start.2
where the time goes:
time: 123 us; the launch traced here: 122 us
  blocking collectives  76.3 us (62%)
  local copies, waits for them, and re-layouts  23.5 us (19%)
  matrix products  10.1 us (8%)
  starting transfers between devices  7.44 us (6%)
  other arithmetic  4.65 us (4%)
    all_gather x1, blocking collectives, joined_rows(): all_ids = lax.all_gather(patch_of_row, 'blk', tiled=True)  33.5 us
    all_gather x1, blocking collectives, local(): all_queries = lax.all_gather(queries, 'blk', tiled=True)  22.9 us
    all_to_all x1, blocking collectives, local(): lax.all_to_all(payload, 'blk', split_axis=0, concat_axis=0, tiled=True)  19.8 us
    all_to_all x1, starting transfers between devices, joined_rows(): lax.all_to_all(tokens.reshape(per_peer, cycle_size, model_width), 'blk',...  7.44 us
    mul x3, local copies, waits for them, and re-layouts, local(): accum = jnp.sum(part_sums * factor[..., None], axis=0)  4.08 us
    reshape x1, local copies, waits for them, and re-layouts, joined_rows(): tokens.reshape(per_peer, cycle_size, model_width)  2.98 us
    dot_general x1, matrix products, local(): jnp.einsum('lhk,khd->lhd', weights.astype(jnp.bfloat16), value_heads, pre...  2.89 us
    gather x1, local copies, waits for them, and re-layouts, joined_rows(): received.reshape(tok_rows, model_width)[inverse]  2.79 us
  transfers between devices with their start and end apart: 1, of which 0 were waited for; matrix products, arithmetic and copies ran while one was open for 5% of the time, Pallas kernels for 0%

commit v1 on v0

--- a/solution.py
+++ b/solution.py
@@ -20,7 +20,12 @@
     tok_rows, model_width = tokens.shape
     per_peer = tok_rows // cycle_size
     patches_dev = tok_rows // CONTRASTS
-    all_ids = lax.all_gather(patch_of_row, "blk", tiled=True)
+    ring = [patch_of_row]
+    for hop in range(15):
+        ring.append(lax.ppermute(ring[-1], "blk", [(dev, (dev + 1) % 16) for dev in range(16)]))
+    all_ids = jnp.roll(
+        jnp.concatenate(ring[::-1], axis=0), (lax.axis_index("blk") + 1) * ring[0].shape[0], axis=0
+    )
     received = lax.all_to_all(
         tokens.reshape(per_peer, cycle_size, model_width),
         "blk",

time: 123 us -> 174 us (1.41)
  waiting for transfers between devices: 0.01 us -> 88 us
  blocking collectives: 76.3 us -> 39.3 us
    ppermute x0 -> x15, waiting for transfers between devices: none -> 88 us  [joined_rows(): lax.ppermute(ring[-1], 'blk', [(dev, (dev + 1) % 16) for dev in range(16)])]
    all_gather x1 -> x0, blocking collectives: 33.5 us -> none  [joined_rows(): all_ids = lax.all_gather(patch_of_row, 'blk', tiled=True)]
    all_gather x1, blocking collectives: 22.9 us -> 19.4 us  [local(): all_queries = lax.all_gather(queries, 'blk', tiled=True)]
  transfers between devices with their start and end apart: 1 -> 16, of which waited for: 0 -> 13; matrix products, arithmetic and copies ran while one was open for 5% -> 5% of each run, Pallas kernels for 0% -> 0%
where the time goes in v1:
time: 174 us; the launch traced here: 173 us
  waiting for transfers between devices  88 us (51%)
  blocking collectives  39.3 us (23%)
  local copies, waits for them, and re-layouts  23.6 us (14%)
  matrix products  10 us (6%)
  starting transfers between devices  7.06 us (4%)
  other arithmetic  4.58 us (3%)
    ppermute x15, waiting for transfers between devices, joined_rows(): lax.ppermute(ring[-1], 'blk', [(dev, (dev + 1) % 16) for dev in range(16)])  88 us
    all_to_all x1, blocking collectives, local(): lax.all_to_all(payload, 'blk', split_axis=0, concat_axis=0, tiled=True)  19.8 us
    all_gather x1, blocking collectives, local(): all_queries = lax.all_gather(queries, 'blk', tiled=True)  19.4 us
    all_to_all x1, starting transfers between devices, joined_rows(): lax.all_to_all(tokens.reshape(per_peer, cycle_size, model_width), 'blk',...  6 us
    mul x3, local copies, waits for them, and re-layouts, local(): accum = jnp.sum(part_sums * factor[..., None], axis=0)  4.07 us
  transfers between devices with their start and end apart: 16, of which 13 were waited for; matrix products, arithmetic and copies ran while one was open for 5% of the time, Pallas kernels for 0%

profile of v1, /device:TPU:0, one launch (start us, length us, event | category | flops | bytes accessed | tf_op | source)
XLA Modules:
  0.0 173.2 jit_solution(5614786078349021345)
XLA Ops:
  0.5 6.5 %collective-permute-done = s32[512]{0:T(512)S(1)} collective-permute-done((s32[512]{0:T(512)}, s32[512]{0:T(512)S(1)}, u32[]{:S(2)}, u32[]{:S(2)}) %collective-permute-start) | collective-permute-done | bytes 2080 | tf_op jit(solution)/shard_map/ppermute | solution.py:25
  6.9 5.7 %collective-permute-done.1 = s32[512]{0:T(512)S(1)} collective-permute-done((s32[512]{0:T(512)S(1)}, s32[512]{0:T(512)S(1)}, u32[]{:S(2)}, u32[]{:S(2)}) %collective-permute-start.1) | collective-permute-done | bytes 2080 | tf_op jit(solution)/shard_map/ppermute | solution.py:25
  12.6 5.7 %collective-permute-done.2 = s32[512]{0:T(512)S(1)} collective-permute-done((s32[512]{0:T(512)S(1)}, s32[512]{0:T(512)S(1)}, u32[]{:S(2)}, u32[]{:S(2)}) %collective-permute-start.2) | collective-permute-done | bytes 2080 | tf_op jit(solution)/shard_map/ppermute | solution.py:25
  18.3 5.7 %collective-permute-done.3 = s32[512]{0:T(512)S(1)} collective-permute-done((s32[512]{0:T(512)S(1)}, s32[512]{0:T(512)S(1)}, u32[]{:S(2)}, u32[]{:S(2)}) %collective-permute-start.3) | collective-permute-done | bytes 2080 | tf_op jit(solution)/shard_map/ppermute | solution.py:25
  24.1 5.7 %collective-permute-done.4 = s32[512]{0:T(512)S(1)} collective-permute-done((s32[512]{0:T(512)S(1)}, s32[512]{0:T(512)S(1)}, u32[]{:S(2)}, u32[]{:S(2)}) %collective-permute-start.4) | collective-permute-done | bytes 2080 | tf_op jit(solution)/shard_map/ppermute | solution.py:25
  29.8 5.7 %collective-permute-done.5 = s32[512]{0:T(512)S(1)} collective-permute-done((s32[512]{0:T(512)S(1)}, s32[512]{0:T(512)S(1)}, u32[]{:S(2)}, u32[]{:S(2)}) %collective-permute-start.5) | collective-permute-done | bytes 2080 | tf_op jit(solution)/shard_map/ppermute | solution.py:25
  35.5 5.7 %collective-permute-done.6 = s32[512]{0:T(512)S(1)} collective-permute-done((s32[512]{0:T(512)S(1)}, s32[512]{0:T(512)S(1)}, u32[]{:S(2)}, u32[]{:S(2)}) %collective-permute-start.6) | collective-permute-done | bytes 2080 | tf_op jit(solution)/shard_map/ppermute | solution.py:25
  41.2 5.7 %collective-permute-done.7 = s32[512]{0:T(512)S(1)} collective-permute-done((s32[512]{0:T(512)S(1)}, s32[512]{0:T(512)S(1)}, u32[]{:S(2)}, u32[]{:S(2)}) %collective-permute-start.7) | collective-permute-done | bytes 2080 | tf_op jit(solution)/shard_map/ppermute | solution.py:25
  46.9 5.7 %collective-permute-done.8 = s32[512]{0:T(512)S(1)} collective-permute-done((s32[512]{0:T(512)S(1)}, s32[512]{0:T(512)S(1)}, u32[]{:S(2)}, u32[]{:S(2)}) %collective-permute-start.8) | collective-permute-done | bytes 2080 | tf_op jit(solution)/shard_map/ppermute | solution.py:25
  52.6 5.7 %collective-permute-done.9 = s32[512]{0:T(512)S(1)} collective-permute-done((s32[512]{0:T(512)S(1)}, s32[512]{0:T(512)S(1)}, u32[]{:S(2)}, u32[]{:S(2)}) %collective-permute-start.9) | collective-permute-done | bytes 2080 | tf_op jit(solution)/shard_map/ppermute | solution.py:25
  58.3 2.8 %copy.62 = bf16[32,16,1024]{2,0,1:T(8,128)(2,1)} copy(bf16[32,16,1024]{2,1,0:T(8,128)(2,1)} %bitcast.58) | data formatting | bytes 2097152 | tf_op jit(solution)/shard_map/reshape | solution.py:30
  61.1 6.0 %all-to-all-start = ((bf16[32,16,1024]{2,0,1:T(8,128)(2,1)}), bf16[32,16,1024]{2,0,1:T(8,128)(2,1)}, u32[]{:S(2)}, u32[]{:S(2)}) async-start(bf16[32,16,1024]{2,0,1:T(8,128)(2,1)} %copy.62), calls=%async_computation | async-start | bytes 2097152 | tf_op jit(solution)/shard_map/all_to_all | solution.py:29
  67.6 2.0 %fusion.5 = bf16[16,1024]{1,0:T(8,128)(2,1)S(1)} fusion(bf16[16,1024]{1,0:T(8,128)(2,1)S(1)} %copy-done.5, bf16[1024,1024]{1,0:T(8,128)(2,1)} %param.14), kind=kOutput, calls=%fused_computation.15 | convolution fusion | flops 33587200 | bytes 2162688 | tf_op jit(solution)/shard_map/dot_general | solution.py:67
  69.6 20.0 %collective-permute-done.11 = s32[512]{0:T(512)S(1)} collective-permute-done((s32[512]{0:T(512)S(1)}, s32[512]{0:T(512)S(1)}, u32[]{:S(2)}, u32[]{:S(2)}) %collective-permute-start.11) | collective-permute-done | bytes 2080 | tf_op jit(solution)/shard_map/ppermute | solution.py:25
  89.6 19.4 %all_gather.3 = bf16[256,1024]{1,0:T(8,128)(2,1)S(1)} all-gather(bf16[16,1024]{1,0:T(8,128)(2,1)S(1)} %fusion.5), channel_id=1, replica_groups=mesh['grp'=2,'blk'=16] {'blk'}, dimensions={0}, use_global_device_ids=true | all-gather | bytes 557056 | tf_op jit(solution)/shard_map/all_gather | solution.py:69
  109.2 5.5 %collective-permute-done.13 = s32[512]{0:T(512)S(1)} collective-permute-done((s32[512]{0:T(512)S(1)}, s32[512]{0:T(512)S(1)}, u32[]{:S(2)}, u32[]{:S(2)}) %collective-permute-start.13) | collective-permute-done | bytes 2080 | tf_op jit(solution)/shard_map/ppermute | solution.py:25
  115.8 4.6 %collective-permute-done.14 = s32[512]{0:T(512)S(1)} collective-permute-done((s32[512]{0:T(512)S(1)}, s32[512]{0:T(512)S(1)}, u32[]{:S(2)}, u32[]{:S(2)}) %collective-permute-start.14) | collective-permute-done | bytes 2080 | tf_op jit(solution)/shard_map/ppermute | solution.py:25
  121.8 2.4 %scatter_custom_fusion = s32[512]{0:T(512)S(1)} fusion(s32[512]{0:T(512)S(1)} %bitcast.61, s32[512]{0:T(512)S(1)} %iota.19, s32[]{:T(128)} %constant.32.clone.1), kind=kCustom, calls=%fused_computation.91 | custom fusion | bytes 2052 | tf_op jit(solution)/shard_map/scatter | solution.py:49
  126.1 2.8 %gather_fusion = bf16[512,1024]{1,0:T(8,128)(2,1)} fusion(bf16[512,1024]{1,0:T(8,128)(2,1)S(1)} %bitcast.52, s32[1024]{0:T(1024)S(1)} %pad_clamp_fusion), kind=kCustom, calls=%fused_computation | custom fusion | bytes 2099200 | tf_op jit(solution)/shard_map/gather | solution.py:51
  135.9 2.9 %fusion.4 = bf16[256,16,64]{0,2,1:T(8,128)(2,1)} fusion(bf16[128,16,64]{0,2,1:T(8,128)(2,1)S(1)} %bitcast.60, f32[16,128,256]{2,1,0:T(8,128)} %copy-done.1, f32[256,16]{0,1:T(8,128)S(1)} %convert_add_fusion), kind=kOutput, calls=%fused_computation.10 | convolution fusion | flops 68419584 | bytes 2899968 | tf_op jit(solution)/shard_map/lhk,khd->lhd/dot_general | solution.py:87
  139.3 2.0 %copy.69 = bf16[256,16,64]{2,1,0:T(8,128)(2,1)S(1)} copy(bf16[256,16,64]{0,2,1:T(8,128)(2,1)} %fusion.4) | data formatting | bytes 1048576 | tf_op jit(solution)/shard_map/convert_element_type | solution.py:97
  143.9 19.8 %all_to_all.10 = bf16[16,16,1088]{2,1,0:T(8,128)(2,1)S(1)} all-to-all(bf16[16,16,1088]{2,1,0:T(8,128)(2,1)S(1)} %pad_maximum_fusion), channel_id=1, replica_groups=mesh['grp'=2,'blk'=16] {'blk'}, dimensions={0} | all-to-all | bytes 1114112 | tf_op jit(solution)/shard_map/all_to_all | solution.py:99
  167.4 2.0 %mul.118 = f32[16,16,1024]{2,1,0:T(8,128)S(1)} reshape(f32[16,16,16,64]{3,2,1,0:T(8,128)} %mul.117) | data formatting | bytes 2097152 | tf_op jit(solution)/shard_map/mul | solution.py:115
  170.6 2.6 %fusion.6 = bf16[16,1024]{1,0:T(8,128)(2,1)} fusion(bf16[1024,1024]{1,0:T(8,128)(2,1)} %param.17, bf16[16,1024]{1,0:T(8,128)(2,1)S(1)} %copy-done.5, f32[16,1024]{1,0:T(8,128)S(1)} %multiply_reduce_fusion, f32[16,1024]{1,0:T(8,128)S(1)} %div.36), kind=kOutput, calls=%fused_computation.16 | convolution fusion | flops 33636352 | bytes 2293760 | tf_op jit(solution)/shard_map/dot_general | solution.py:117
  (114 shorter events, 19.8 us)
Async XLA Ops:
  0.0 130.5 %copy-start = (bf16[1024,1024]{1,0:T(8,128)(2,1)S(1)}, bf16[1024,1024]{1,0:T(8,128)(2,1)}, u32[]{:S(2)}) copy-start(bf16[1024,1024]{1,0:T(8,128)(2,1)} %param.15) | copy-start | bytes 6291460
  0.0 6.9 %collective-permute-start = (s32[512]{0:T(512)}, s32[512]{0:T(512)S(1)}, u32[]{:S(2)}, u32[]{:S(2)}) collective-permute-start(s32[512]{0:T(512)} %param.10), channel_id=1, source_target_pairs={{0,1},{1,2},{2,3},{3,4},{4,5},{5,6},{6,7},{7,8},{8,9},{9,10},{10,1... | collective-permute-start | bytes 6152 | tf_op jit(solution)/shard_map/ppermute | solution.py:25
  6.9 5.7 %collective-permute-start.1 = (s32[512]{0:T(512)S(1)}, s32[512]{0:T(512)S(1)}, u32[]{:S(2)}, u32[]{:S(2)}) collective-permute-start(s32[512]{0:T(512)S(1)} %collective-permute-done), channel_id=1, source_target_pairs={{0,1},{1,2},{2,3},{3,4},{4,5},{5,6},{6,7},{7,8},{8,9},{9,10},{10,1... | collective-permute-start | bytes 6152 | tf_op jit(solution)/shard_map/ppermute | solution.py:25
  12.6 5.7 %collective-permute-start.2 = (s32[512]{0:T(512)S(1)}, s32[512]{0:T(512)S(1)}, u32[]{:S(2)}, u32[]{:S(2)}) collective-permute-start(s32[512]{0:T(512)S(1)} %collective-permute-done.1), channel_id=1, source_target_pairs={{0,1},{1,2},{2,3},{3,4},{4,5},{5,6},{6,7},{7,8},{8,9},{9,10},{10,1... | collective-permute-start | bytes 6152 | tf_op jit(solution)/shard_map/ppermute | solution.py:25
  18.3 5.7 %collective-permute-start.3 = (s32[512]{0:T(512)S(1)}, s32[512]{0:T(512)S(1)}, u32[]{:S(2)}, u32[]{:S(2)}) collective-permute-start(s32[512]{0:T(512)S(1)} %collective-permute-done.2), channel_id=1, source_target_pairs={{0,1},{1,2},{2,3},{3,4},{4,5},{5,6},{6,7},{7,8},{8,9},{9,10},{10,1... | collective-permute-start | bytes 6152 | tf_op jit(solution)/shard_map/ppermute | solution.py:25
  24.0 5.7 %collective-permute-start.4 = (s32[512]{0:T(512)S(1)}, s32[512]{0:T(512)S(1)}, u32[]{:S(2)}, u32[]{:S(2)}) collective-permute-start(s32[512]{0:T(512)S(1)} %collective-permute-done.3), channel_id=1, source_target_pairs={{0,1},{1,2},{2,3},{3,4},{4,5},{5,6},{6,7},{7,8},{8,9},{9,10},{10,1... | collective-permute-start | bytes 6152 | tf_op jit(solution)/shard_map/ppermute | solution.py:25
  29.8 5.7 %collective-permute-start.5 = (s32[512]{0:T(512)S(1)}, s32[512]{0:T(512)S(1)}, u32[]{:S(2)}, u32[]{:S(2)}) collective-permute-start(s32[512]{0:T(512)S(1)} %collective-permute-done.4), channel_id=1, source_target_pairs={{0,1},{1,2},{2,3},{3,4},{4,5},{5,6},{6,7},{7,8},{8,9},{9,10},{10,1... | collective-permute-start | bytes 6152 | tf_op jit(solution)/shard_map/ppermute | solution.py:25
  35.5 5.7 %collective-permute-start.6 = (s32[512]{0:T(512)S(1)}, s32[512]{0:T(512)S(1)}, u32[]{:S(2)}, u32[]{:S(2)}) collective-permute-start(s32[512]{0:T(512)S(1)} %collective-permute-done.5), channel_id=1, source_target_pairs={{0,1},{1,2},{2,3},{3,4},{4,5},{5,6},{6,7},{7,8},{8,9},{9,10},{10,1... | collective-permute-start | bytes 6152 | tf_op jit(solution)/shard_map/ppermute | solution.py:25
  41.2 5.7 %collective-permute-start.7 = (s32[512]{0:T(512)S(1)}, s32[512]{0:T(512)S(1)}, u32[]{:S(2)}, u32[]{:S(2)}) collective-permute-start(s32[512]{0:T(512)S(1)} %collective-permute-done.6), channel_id=1, source_target_pairs={{0,1},{1,2},{2,3},{3,4},{4,5},{5,6},{6,7},{7,8},{8,9},{9,10},{10,1... | collective-permute-start | bytes 6152 | tf_op jit(solution)/shard_map/ppermute | solution.py:25
  46.9 5.7 %collective-permute-start.8 = (s32[512]{0:T(512)S(1)}, s32[512]{0:T(512)S(1)}, u32[]{:S(2)}, u32[]{:S(2)}) collective-permute-start(s32[512]{0:T(512)S(1)} %collective-permute-done.7), channel_id=1, source_target_pairs={{0,1},{1,2},{2,3},{3,4},{4,5},{5,6},{6,7},{7,8},{8,9},{9,10},{10,1... | collective-permute-start | bytes 6152 | tf_op jit(solution)/shard_map/ppermute | solution.py:25
  52.6 5.7 %collective-permute-start.9 = (s32[512]{0:T(512)S(1)}, s32[512]{0:T(512)S(1)}, u32[]{:S(2)}, u32[]{:S(2)}) collective-permute-start(s32[512]{0:T(512)S(1)} %collective-permute-done.8), channel_id=1, source_target_pairs={{0,1},{1,2},{2,3},{3,4},{4,5},{5,6},{6,7},{7,8},{8,9},{9,10},{10,1... | collective-permute-start | bytes 6152 | tf_op jit(solution)/shard_map/ppermute | solution.py:25
  58.3 8.9 %collective-permute-start.10 = (s32[512]{0:T(512)S(1)}, s32[512]{0:T(512)S(1)}, u32[]{:S(2)}, u32[]{:S(2)}) collective-permute-start(s32[512]{0:T(512)S(1)} %collective-permute-done.9), channel_id=1, source_target_pairs={{0,1},{1,2},{2,3},{3,4},{4,5},{5,6},{6,7},{7,8},{8,9},{9,10},{10,1... | collective-permute-start | bytes 6152 | tf_op jit(solution)/shard_map/ppermute | solution.py:25
  58.3 9.3 %copy-start.5 = (bf16[16,1024]{1,0:T(8,128)(2,1)S(1)}, bf16[16,1024]{1,0:T(8,128)(2,1)}, u32[]{:S(2)}) copy-start(bf16[16,1024]{1,0:T(8,128)(2,1)} %param.11) | copy-start | bytes 98308
  61.1 53.6 %copy-start.8 = (bf16[1024]{0:T(1024)(128)(2,1)S(1)}, bf16[1024]{0:T(1024)(128)(2,1)}, u32[]{:S(2)}) copy-start(bf16[1024]{0:T(1024)(128)(2,1)} %param.13) | copy-start | bytes 6148
  61.1 53.7 %copy-start.6 = (bf16[4,1024]{1,0:T(4,128)(2,1)S(1)}, bf16[4,1024]{1,0:T(4,128)(2,1)}, u32[]{:S(2)}) copy-start(bf16[4,1024]{1,0:T(4,128)(2,1)} %param.12) | copy-start | bytes 24580
  61.1 63.1 %all-to-all-start = ((bf16[32,16,1024]{2,0,1:T(8,128)(2,1)}), bf16[32,16,1024]{2,0,1:T(8,128)(2,1)}, u32[]{:S(2)}, u32[]{:S(2)}) async-start(bf16[32,16,1024]{2,0,1:T(8,128)(2,1)} %copy.62), calls=%async_computation | async-start | bytes 2097152 | tf_op jit(solution)/shard_map/all_to_all | solution.py:29
  67.1 53.5 %copy-start.7 = (s32[512]{0:T(512)S(1)}, s32[512]{0:T(512)}, u32[]{:S(2)}) copy-start(s32[512]{0:T(512)} %param.10) | copy-start | bytes 6148
  67.2 22.4 %collective-permute-start.11 = (s32[512]{0:T(512)S(1)}, s32[512]{0:T(512)S(1)}, u32[]{:S(2)}, u32[]{:S(2)}) collective-permute-start(s32[512]{0:T(512)S(1)} %collective-permute-done.10), channel_id=1, source_target_pairs={{0,1},{1,2},{2,3},{3,4},{4,5},{5,6},{6,7},{7,8},{8,9},{9,10},{10,1... | collective-permute-start | bytes 6152 | tf_op jit(solution)/shard_map/ppermute | solution.py:25
  89.6 19.4 %collective-permute-start.12 = (s32[512]{0:T(512)S(1)}, s32[512]{0:T(512)S(1)}, u32[]{:S(2)}, u32[]{:S(2)}) collective-permute-start(s32[512]{0:T(512)S(1)} %collective-permute-done.11), channel_id=1, source_target_pairs={{0,1},{1,2},{2,3},{3,4},{4,5},{5,6},{6,7},{7,8},{8,9},{9,10},{10,1... | collective-permute-start | bytes 6152 | tf_op jit(solution)/shard_map/ppermute | solution.py:25
  109.0 5.7 %collective-permute-start.13 = (s32[512]{0:T(512)S(1)}, s32[512]{0:T(512)S(1)}, u32[]{:S(2)}, u32[]{:S(2)}) collective-permute-start(s32[512]{0:T(512)S(1)} %collective-permute-done.12), channel_id=1, source_target_pairs={{0,1},{1,2},{2,3},{3,4},{4,5},{5,6},{6,7},{7,8},{8,9},{9,10},{10,1... | collective-permute-start | bytes 6152 | tf_op jit(solution)/shard_map/ppermute | solution.py:25
  114.7 5.7 %collective-permute-start.14 = (s32[512]{0:T(512)S(1)}, s32[512]{0:T(512)S(1)}, u32[]{:S(2)}, u32[]{:S(2)}) collective-permute-start(s32[512]{0:T(512)S(1)} %collective-permute-done.13), channel_id=1, source_target_pairs={{0,1},{1,2},{2,3},{3,4},{4,5},{5,6},{6,7},{7,8},{8,9},{9,10},{10,1... | collective-permute-start | bytes 6152 | tf_op jit(solution)/shard_map/ppermute | solution.py:25
  130.4 1.5 copy-start.4
  131.9 3.3 %copy-start.3 = (bf16[1024,1024]{1,0:T(8,128)(2,1)S(1)}, bf16[1024,1024]{1,0:T(8,128)(2,1)}, u32[]{:S(2)}) copy-start(bf16[1024,1024]{1,0:T(8,128)(2,1)} %param.16) | copy-start | bytes 6291460
  133.5 1.3 copy-start.1
  (1 other events, 0.8 us)
